TPU v7x, 256 devices: a whole 4x4x8 slice. The times are simulated.
256 devices in a mesh: ctx: 32 (over x, y, core), tp: 8 (over z).
Axes of the slice: x: 4, y: 4, z: 8, core: 2. Of those that a mesh axis runs over, the one named last changes fastest.
Arguments:
- hidden_states: bfloat16 [65536, 4096], P('ctx', 'tp')
- chosen: int32 [12288], P('ctx'), may hold values from 0 to 2048, as said below
- router_gate: float32 [12288], P('ctx'), may hold values from 0.2 to 1
- w_query: bfloat16 [4096, 4096], P(None, 'tp'), may hold values from -0.09375 to 0.09375
- w_key: bfloat16 [4096, 1024], P(None, 'tp'), may hold values from -0.09375 to 0.09375
- w_value: bfloat16 [4096, 1024], P(None, 'tp'), may hold values from -0.09375 to 0.09375
Outputs:
- attended: bfloat16 [12288, 4096], P('ctx', 'tp')
Inputs may be any that keep to these rules, and one draw needn't show every extreme that they name: `chosen`: each shard's 384 slots hold the sorted distinct positions of its routed tokens, then 2048 in every unused slot; a shard routes from 128 to 384 tokens, some shard exactly 384, and all shards together 65536 // 8.
All inputs are finite; a program needn't handle non-finite values.
Results may differ from a plain program's by a relative error of at most 0.035.
Values may be sent and summed in bfloat16 or wider, within the bound.
No kernel may reach another device: no remote copies, remote signals or barrier semaphores. Data moves between devices by JAX's collectives and lax.ppermute only.
A program may use at most 64 MiB of HBM per device.

v0:
```python
import math

import jax
import jax.numpy as jnp
from jax import lax
from jax.sharding import PartitionSpec as P

HEAD_DIM = 128


ROPE_BASE = 500000.0
MASKED = -1e30


def rotate(values_in, position):
    half_dim = values_in.shape[-1] // 2
    frequency = jnp.exp(
        jnp.arange(half_dim, dtype=jnp.float32) * (-2.0 * math.log(ROPE_BASE) / values_in.shape[-1])
    )
    angles = position.astype(jnp.float32)[:, None] * frequency[None, :]
    cosine = jnp.cos(angles)[:, None, :]
    sine = jnp.sin(angles)[:, None, :]
    first = values_in[..., :half_dim]
    second = values_in[..., half_dim:]
    return jnp.concatenate(
        [first * cosine - second * sine, second * cosine + first * sine], axis=-1
    )


def empty_state(count, kv_local, group, head_dim):
    return (
        jnp.full((kv_local, group, count), MASKED, jnp.float32),
        jnp.zeros((kv_local, group, count), jnp.float32),
        jnp.zeros((count, kv_local, group, head_dim), jnp.float32),
    )


def update(state, queries, query_pos, key_block, value_block, key_pos):
    running, totals, summed = state
    scores = jnp.einsum("rhgd,khd->hgrk", queries, key_block, preferred_element_type=jnp.float32)
    allowed = key_pos[None, None, None, :] <= query_pos[None, None, :, None]
    newest = jnp.maximum(running, jnp.max(jnp.where(allowed, scores, MASKED), axis=-1))
    factor = jnp.exp(running - newest)
    weights = jnp.where(allowed, jnp.exp(scores - newest[..., None]), 0.0)
    totals = totals * factor + jnp.sum(weights, axis=-1)
    mixed = jnp.einsum(
        "hgrk,khd->rhgd",
        weights.astype(jnp.bfloat16),
        value_block,
        preferred_element_type=jnp.float32,
    )
    summed = summed * jnp.transpose(factor, (2, 0, 1))[..., None] + mixed
    return (newest, totals, summed)


def finish(state):
    running, totals, summed = state
    denom = jnp.where(totals > 0.0, totals, 1.0)
    return summed / jnp.transpose(denom, (2, 0, 1))[..., None]


def highest(position, pad_mark):
    return jnp.max(jnp.where(position < pad_mark, position, -1))


def fold_keys(states, pieces, groups):
    key_rows, value_rows, key_pos = pieces
    length = key_rows.shape[0]
    block_rows = length
    for size_rows in (1536, 768, 384):
        block_rows = size_rows
        break
    blocks = length // block_rows
    shaped = (
        key_rows.reshape((blocks, block_rows) + key_rows.shape[1:]),
        value_rows.reshape((blocks, block_rows) + value_rows.shape[1:]),
        key_pos.reshape(blocks, block_rows),
    )

    def advance(carried, block):
        key_block, value_block, block_pos = block
        fresh = []
        for state, group_data in zip(carried, groups):
            queries, query_pos, limit = group_data

            def visit(current):
                return update(current, queries, query_pos, key_block, value_block, block_pos)

            def keep_state(current):
                return current

            fresh.append(lax.cond(jnp.min(block_pos) > limit, keep_state, visit, state))
        return (tuple(fresh), None)

    result, unused = lax.scan(advance, tuple(states), shaped)
    return result


def body(hidden_states, chosen, router_gate, w_query, w_key, w_value):
    seq_rows = hidden_states.shape[0]
    slot_count = chosen.shape[0]
    head_dim = HEAD_DIM
    query_width = w_query.shape[1]
    kv_width = w_key.shape[1]
    kv_local = kv_width // head_dim
    heads_local = query_width // head_dim
    group = heads_local // kv_local
    live = chosen < seq_rows
    pad_mark = lax.axis_size("ctx") * seq_rows + 1
    position = jnp.where(live, lax.axis_index("ctx") * seq_rows + chosen, pad_mark)
    picked = hidden_states[jnp.minimum(chosen, seq_rows - 1)]
    gated = jnp.where(live, router_gate, 0.0)
    piece = lax.all_gather(picked, "tp", axis=1, tiled=True)
    query_part = jnp.dot(piece, w_query, preferred_element_type=jnp.float32)
    key_part = jnp.dot(piece, w_key, preferred_element_type=jnp.float32)
    value_part = jnp.dot(piece, w_value, preferred_element_type=jnp.float32)
    queries = (
        rotate(query_part.reshape(slot_count, heads_local, head_dim), position) * head_dim ** (-0.5)
    ).astype(jnp.bfloat16)
    queries = queries.reshape(slot_count, kv_local, group, head_dim)
    key_rows = rotate(key_part.reshape(slot_count, kv_local, head_dim), position).astype(
        jnp.bfloat16
    )
    value_rows = value_part.reshape(slot_count, kv_local, head_dim).astype(jnp.bfloat16)
    groups = [(queries, position, highest(position, pad_mark))]
    states = fold_keys(
        (empty_state(slot_count, kv_local, group, head_dim),),
        (
            lax.all_gather(key_rows, "ctx", axis=0, tiled=True),
            lax.all_gather(value_rows, "ctx", axis=0, tiled=True),
            lax.all_gather(position, "ctx", axis=0, tiled=True),
        ),
        groups,
    )
    result = (finish(states[0]) * gated[:, None, None, None]).astype(jnp.bfloat16)
    return result.reshape(slot_count, query_width)


def solution(mesh):
    placed = (P("ctx", "tp"), P("ctx"), P("ctx"), P(None, "tp"), P(None, "tp"), P(None, "tp"))
    return jax.shard_map(
        body, mesh=mesh, in_specs=placed, out_specs=P("ctx", "tp"), check_vma=False
    )
```

profile of v0, /device:TPU:31, one launch (start us, length us, event | category | flops | bytes accessed | tf_op | source)
XLA Modules:
  0.0 253.2 jit_solution(8523070852562474726)
XLA Ops:
  8.1 2.6 %gather_fusion = bf16[384,512]{1,0:T(8,128)(2,1)} fusion(bf16[2048,512]{1,0:T(8,128)(2,1)S(1)} %copy-done, s32[1024]{0:T(1024)S(1)} %pad_clamp_fusion), kind=kCustom, calls=%fused_computation | custom fusion | bytes 787968 | tf_op jit(solution)/shard_map/gather | solution.py:111
  10.8 47.2 %all-gather.9.cloned.1.call-done = bf16[384,4096]{1,0:T(8,128)(2,1)} async-done(((bf16[384,512]{1,0:T(8,128)(2,1)}), bf16[384,4096]{1,0:T(8,128)(2,1)}) %all-gather.9.cloned.1.call-update) | async-done | bytes 3145744 | tf_op jit(solution)/shard_map/all_gather | solution.py:113
  58.0 3.5 %convolution_convert_fusion = bf16[384,128]{1,0:T(8,128)(2,1)} fusion(bf16[384,4096]{1,0:T(8,128)(2,1)} %all-gather.9.cloned.1.call-done, bf16[4096,128]{1,0:T(8,128)(2,1)S(1)} %copy-done.1), kind=kOutput, calls=%fused_computation.29 | convolution fusion | flops 402702336 | bytes 4292608 | tf_op jit(solution)/shard_map/dot_general | solution.py:116
  61.6 3.2 %convolution_bitcast_fusion = f32[384,1,128]{0,2,1:T(8,128)S(1)} fusion(bf16[384,4096]{1,0:T(8,128)(2,1)} %all-gather.9.cloned.1.call-done, bf16[4096,128]{1,0:T(8,128)(2,1)} %param.14), kind=kOutput, calls=%fused_computation.28 | convolution fusion | flops 402653184 | bytes 4390912 | tf_op jit(solution)/shard_map/dot_general | solution.py:115
  65.9 23.3 %all-gather.2 = s32[32,1,384]{2,1,0:T(1,128)S(1)} all-gather(s32[1,1,384]{2,1,0:T(1,128)S(1)} %reshape.287), channel_id=1, replica_groups=mesh['ctx'=32,'tp'=8] {'ctx'}, dimensions={0}, use_global_device_ids=true | all-gather | bytes 50688 | tf_op jit(solution)/shard_map/all_gather | solution.py:131
  90.8 5.8 %fusion.39 = f32[384,512]{1,0:T(8,128)} fusion(bf16[384,4096]{1,0:T(8,128)(2,1)} %all-gather.9.cloned.1.call-done, bf16[4096,512]{1,0:T(8,128)(2,1)} %param.13), kind=kOutput, calls=%fused_computation.61 | convolution fusion | flops 1610612736 | bytes 8126464 | tf_op jit(solution)/shard_map/dot_general | solution.py:114
  98.9 10.0 %all-gather.11.cloned.1.call-done = bf16[12288,128]{1,0:T(8,128)(2,1)} async-done(((bf16[384,128]{1,0:T(8,128)(2,1)}), bf16[12288,128]{1,0:T(8,128)(2,1)}) %all-gather.11.cloned.1.call-update) | async-done | bytes 3145744 | tf_op jit(solution)/shard_map/all_gather | solution.py:130
  108.9 4.6 %copy.17 = bf16[8,1536,1,128]{1,3,2,0:T(8,128)(2,1)} copy(bf16[8,1536,1,128]{3,1,0,2:T(8,128)(2,1)} %bitcast.82) | data formatting | bytes 6291456 | tf_op jit(solution)/shard_map/while | solution.py:95
  113.5 48.9 %all-gather.7.cloned.1.call-done = bf16[12288,1,128]{0,2,1:T(8,128)(2,1)} async-done(((bf16[384,1,128]{0,2,1:T(8,128)(2,1)}), bf16[12288,1,128]{0,2,1:T(8,128)(2,1)}) %all-gather.7.cloned.1.call-update) | async-done | bytes 3145744 | tf_op jit(solution)/shard_map/all_gather | solution.py:129
  162.4 4.6 %copy.20 = bf16[12288,1,128]{2,0,1:T(8,128)(2,1)} copy(bf16[12288,1,128]{0,2,1:T(8,128)(2,1)} %all-gather.7.cloned.1.call-done) | data formatting | bytes 6291456 | tf_op jit(solution)/shard_map/while | solution.py:95
  167.1 78.5 %while.14 = (s32[]{:T(128)}, f32[1,4,384]{2,1,0:T(4,128)S(1)}, f32[1,4,384]{2,1,0:T(4,128)S(1)}, f32[384,1,4,128]{0,3,2,1:T(8,128)S(1)}, s32[8,1536]{1,0:T(8,128...) while((s32[]{:T(128)}, f32[1,4,384]{2,1,0:T(4,128)S(1)}, ...), condition=%wide.region_7.8_spmd, body=%wide.region_1.7_spmd.sunk | while | flops 1227823104 | bytes 33555200 | solution.py:95
  169.0 7.8 %conditional.2 = (f32[1,4,384]{2,1,0:T(4,128)S(1)}, f32[1,4,384]{2,1,0:T(4,128)S(1)}, f32[384,1,4,128]{0,3,2,1:T(8,128)S(1)}) conditional(s32[]{:T(128)} %convert_element_type.58, (s32[1,1536]{1,0:T(1,128)S(1)}, s32[384]{0:T(512)S(1)}, bf16[8,1536,1,128]{3,1,2,0:T(8,128)(2,1)}, s32[]{:T(128)}, bf16[384,1,4,128]{3,0,2,1:T(8,128)(2,1)S(1)}, ...), branch_computations={%region_3.5_spmd, %region_6.6_spmd} | conditional | flops 1227821568 | bytes 33530396 | solution.py:92
  169.5 2.5 fusion
  173.7 3.2 %fusion.12 = f32[384,1,4,128]{0,3,2,1:T(8,128)S(1)} fusion(f32[1536,384,4]{1,0,2:T(8,128)S(1)} %get-tuple-element.191, f32[4,384]{1,0:T(4,128)S(1)} %bitcast.84, pred[384,1536]{0,1:T(8,128)(4,1)S(1)} %broadcast_compare_fusion, f32[384,1,4,128]{0,3,2,1:T(8,128)S(1)} %get-tuple-element.124, bf16[8,1536,1,128]{1,3,2,0:T(8,128)(2,1)} %get-tuple-element.125, ...), kind=kOutput, calls=%fused_computation.12 | convolution fusion | flops 611450880 | bytes 12005888 | tf_op jit(solution)/shard_map/while/body/eval_jaxpr/cond/branch_0_fun/hgrk,khd->rhgd/dot_general | solution.py:46
  178.8 7.9 %conditional.2 = (f32[1,4,384]{2,1,0:T(4,128)S(1)}, f32[1,4,384]{2,1,0:T(4,128)S(1)}, f32[384,1,4,128]{0,3,2,1:T(8,128)S(1)}) conditional(s32[]{:T(128)} %convert_element_type.58, (s32[1,1536]{1,0:T(1,128)S(1)}, s32[384]{0:T(512)S(1)}, bf16[8,1536,1,128]{3,1,2,0:T(8,128)(2,1)}, s32[]{:T(128)}, bf16[384,1,4,128]{3,0,2,1:T(8,128)(2,1)S(1)}, ...), branch_computations={%region_3.5_spmd, %region_6.6_spmd} | conditional | flops 1227821568 | bytes 33530396 | solution.py:92
  179.3 2.5 fusion
  183.5 3.2 %fusion.12 = f32[384,1,4,128]{0,3,2,1:T(8,128)S(1)} fusion(f32[1536,384,4]{1,0,2:T(8,128)S(1)} %get-tuple-element.191, f32[4,384]{1,0:T(4,128)S(1)} %bitcast.84, pred[384,1536]{0,1:T(8,128)(4,1)S(1)} %broadcast_compare_fusion, f32[384,1,4,128]{0,3,2,1:T(8,128)S(1)} %get-tuple-element.124, bf16[8,1536,1,128]{1,3,2,0:T(8,128)(2,1)} %get-tuple-element.125, ...), kind=kOutput, calls=%fused_computation.12 | convolution fusion | flops 611450880 | bytes 12005888 | tf_op jit(solution)/shard_map/while/body/eval_jaxpr/cond/branch_0_fun/hgrk,khd->rhgd/dot_general | solution.py:46
  188.6 7.9 %conditional.2 = (f32[1,4,384]{2,1,0:T(4,128)S(1)}, f32[1,4,384]{2,1,0:T(4,128)S(1)}, f32[384,1,4,128]{0,3,2,1:T(8,128)S(1)}) conditional(s32[]{:T(128)} %convert_element_type.58, (s32[1,1536]{1,0:T(1,128)S(1)}, s32[384]{0:T(512)S(1)}, bf16[8,1536,1,128]{3,1,2,0:T(8,128)(2,1)}, s32[]{:T(128)}, bf16[384,1,4,128]{3,0,2,1:T(8,128)(2,1)S(1)}, ...), branch_computations={%region_3.5_spmd, %region_6.6_spmd} | conditional | flops 1227821568 | bytes 33530396 | solution.py:92
  189.1 2.5 fusion
  193.3 3.2 %fusion.12 = f32[384,1,4,128]{0,3,2,1:T(8,128)S(1)} fusion(f32[1536,384,4]{1,0,2:T(8,128)S(1)} %get-tuple-element.191, f32[4,384]{1,0:T(4,128)S(1)} %bitcast.84, pred[384,1536]{0,1:T(8,128)(4,1)S(1)} %broadcast_compare_fusion, f32[384,1,4,128]{0,3,2,1:T(8,128)S(1)} %get-tuple-element.124, bf16[8,1536,1,128]{1,3,2,0:T(8,128)(2,1)} %get-tuple-element.125, ...), kind=kOutput, calls=%fused_computation.12 | convolution fusion | flops 611450880 | bytes 12005888 | tf_op jit(solution)/shard_map/while/body/eval_jaxpr/cond/branch_0_fun/hgrk,khd->rhgd/dot_general | solution.py:46
  198.5 7.9 %conditional.2 = (f32[1,4,384]{2,1,0:T(4,128)S(1)}, f32[1,4,384]{2,1,0:T(4,128)S(1)}, f32[384,1,4,128]{0,3,2,1:T(8,128)S(1)}) conditional(s32[]{:T(128)} %convert_element_type.58, (s32[1,1536]{1,0:T(1,128)S(1)}, s32[384]{0:T(512)S(1)}, bf16[8,1536,1,128]{3,1,2,0:T(8,128)(2,1)}, s32[]{:T(128)}, bf16[384,1,4,128]{3,0,2,1:T(8,128)(2,1)S(1)}, ...), branch_computations={%region_3.5_spmd, %region_6.6_spmd} | conditional | flops 1227821568 | bytes 33530396 | solution.py:92
  198.9 2.5 fusion
  203.1 3.2 %fusion.12 = f32[384,1,4,128]{0,3,2,1:T(8,128)S(1)} fusion(f32[1536,384,4]{1,0,2:T(8,128)S(1)} %get-tuple-element.191, f32[4,384]{1,0:T(4,128)S(1)} %bitcast.84, pred[384,1536]{0,1:T(8,128)(4,1)S(1)} %broadcast_compare_fusion, f32[384,1,4,128]{0,3,2,1:T(8,128)S(1)} %get-tuple-element.124, bf16[8,1536,1,128]{1,3,2,0:T(8,128)(2,1)} %get-tuple-element.125, ...), kind=kOutput, calls=%fused_computation.12 | convolution fusion | flops 611450880 | bytes 12005888 | tf_op jit(solution)/shard_map/while/body/eval_jaxpr/cond/branch_0_fun/hgrk,khd->rhgd/dot_general | solution.py:46
  208.3 7.9 %conditional.2 = (f32[1,4,384]{2,1,0:T(4,128)S(1)}, f32[1,4,384]{2,1,0:T(4,128)S(1)}, f32[384,1,4,128]{0,3,2,1:T(8,128)S(1)}) conditional(s32[]{:T(128)} %convert_element_type.58, (s32[1,1536]{1,0:T(1,128)S(1)}, s32[384]{0:T(512)S(1)}, bf16[8,1536,1,128]{3,1,2,0:T(8,128)(2,1)}, s32[]{:T(128)}, bf16[384,1,4,128]{3,0,2,1:T(8,128)(2,1)S(1)}, ...), branch_computations={%region_3.5_spmd, %region_6.6_spmd} | conditional | flops 1227821568 | bytes 33530396 | solution.py:92
  208.7 2.5 fusion
  213.0 3.2 %fusion.12 = f32[384,1,4,128]{0,3,2,1:T(8,128)S(1)} fusion(f32[1536,384,4]{1,0,2:T(8,128)S(1)} %get-tuple-element.191, f32[4,384]{1,0:T(4,128)S(1)} %bitcast.84, pred[384,1536]{0,1:T(8,128)(4,1)S(1)} %broadcast_compare_fusion, f32[384,1,4,128]{0,3,2,1:T(8,128)S(1)} %get-tuple-element.124, bf16[8,1536,1,128]{1,3,2,0:T(8,128)(2,1)} %get-tuple-element.125, ...), kind=kOutput, calls=%fused_computation.12 | convolution fusion | flops 611450880 | bytes 12005888 | tf_op jit(solution)/shard_map/while/body/eval_jaxpr/cond/branch_0_fun/hgrk,khd->rhgd/dot_general | solution.py:46
  218.1 7.9 %conditional.2 = (f32[1,4,384]{2,1,0:T(4,128)S(1)}, f32[1,4,384]{2,1,0:T(4,128)S(1)}, f32[384,1,4,128]{0,3,2,1:T(8,128)S(1)}) conditional(s32[]{:T(128)} %convert_element_type.58, (s32[1,1536]{1,0:T(1,128)S(1)}, s32[384]{0:T(512)S(1)}, bf16[8,1536,1,128]{3,1,2,0:T(8,128)(2,1)}, s32[]{:T(128)}, bf16[384,1,4,128]{3,0,2,1:T(8,128)(2,1)S(1)}, ...), branch_computations={%region_3.5_spmd, %region_6.6_spmd} | conditional | flops 1227821568 | bytes 33530396 | solution.py:92
  222.8 3.2 %fusion.12 = f32[384,1,4,128]{0,3,2,1:T(8,128)S(1)} fusion(f32[1536,384,4]{1,0,2:T(8,128)S(1)} %get-tuple-element.191, f32[4,384]{1,0:T(4,128)S(1)} %bitcast.84, pred[384,1536]{0,1:T(8,128)(4,1)S(1)} %broadcast_compare_fusion, f32[384,1,4,128]{0,3,2,1:T(8,128)S(1)} %get-tuple-element.124, bf16[8,1536,1,128]{1,3,2,0:T(8,128)(2,1)} %get-tuple-element.125, ...), kind=kOutput, calls=%fused_computation.12 | convolution fusion | flops 611450880 | bytes 12005888 | tf_op jit(solution)/shard_map/while/body/eval_jaxpr/cond/branch_0_fun/hgrk,khd->rhgd/dot_general | solution.py:46
  227.9 7.9 %conditional.2 = (f32[1,4,384]{2,1,0:T(4,128)S(1)}, f32[1,4,384]{2,1,0:T(4,128)S(1)}, f32[384,1,4,128]{0,3,2,1:T(8,128)S(1)}) conditional(s32[]{:T(128)} %convert_element_type.58, (s32[1,1536]{1,0:T(1,128)S(1)}, s32[384]{0:T(512)S(1)}, bf16[8,1536,1,128]{3,1,2,0:T(8,128)(2,1)}, s32[]{:T(128)}, bf16[384,1,4,128]{3,0,2,1:T(8,128)(2,1)S(1)}, ...), branch_computations={%region_3.5_spmd, %region_6.6_spmd} | conditional | flops 1227821568 | bytes 33530396 | solution.py:92
  232.6 3.2 %fusion.12 = f32[384,1,4,128]{0,3,2,1:T(8,128)S(1)} fusion(f32[1536,384,4]{1,0,2:T(8,128)S(1)} %get-tuple-element.191, f32[4,384]{1,0:T(4,128)S(1)} %bitcast.84, pred[384,1536]{0,1:T(8,128)(4,1)S(1)} %broadcast_compare_fusion, f32[384,1,4,128]{0,3,2,1:T(8,128)S(1)} %get-tuple-element.124, bf16[8,1536,1,128]{1,3,2,0:T(8,128)(2,1)} %get-tuple-element.125, ...), kind=kOutput, calls=%fused_computation.12 | convolution fusion | flops 611450880 | bytes 12005888 | tf_op jit(solution)/shard_map/while/body/eval_jaxpr/cond/branch_0_fun/hgrk,khd->rhgd/dot_general | solution.py:46
  237.7 7.9 %conditional.2 = (f32[1,4,384]{2,1,0:T(4,128)S(1)}, f32[1,4,384]{2,1,0:T(4,128)S(1)}, f32[384,1,4,128]{0,3,2,1:T(8,128)S(1)}) conditional(s32[]{:T(128)} %convert_element_type.58, (s32[1,1536]{1,0:T(1,128)S(1)}, s32[384]{0:T(512)S(1)}, bf16[8,1536,1,128]{3,1,2,0:T(8,128)(2,1)}, s32[]{:T(128)}, bf16[384,1,4,128]{3,0,2,1:T(8,128)(2,1)S(1)}, ...), branch_computations={%region_3.5_spmd, %region_6.6_spmd} | conditional | flops 1227821568 | bytes 33530396 | solution.py:92
  242.4 3.2 %fusion.12 = f32[384,1,4,128]{0,3,2,1:T(8,128)S(1)} fusion(f32[1536,384,4]{1,0,2:T(8,128)S(1)} %get-tuple-element.191, f32[4,384]{1,0:T(4,128)S(1)} %bitcast.84, pred[384,1536]{0,1:T(8,128)(4,1)S(1)} %broadcast_compare_fusion, f32[384,1,4,128]{0,3,2,1:T(8,128)S(1)} %get-tuple-element.124, bf16[8,1536,1,128]{1,3,2,0:T(8,128)(2,1)} %get-tuple-element.125, ...), kind=kOutput, calls=%fused_computation.12 | convolution fusion | flops 611450880 | bytes 12005888 | tf_op jit(solution)/shard_map/while/body/eval_jaxpr/cond/branch_0_fun/hgrk,khd->rhgd/dot_general | solution.py:46
  (94 shorter events, 37.7 us)
Async XLA Ops:
  6.5 1.6 copy-start
  6.5 51.4 %copy-start.1 = (bf16[4096,128]{1,0:T(8,128)(2,1)S(1)}, bf16[4096,128]{1,0:T(8,128)(2,1)}, u32[]{:S(2)}) copy-start(bf16[4096,128]{1,0:T(8,128)(2,1)} %param.15) | copy-start | bytes 3145732
  6.5 51.4 %all-gather.9.cloned.1.call-start = ((), (), s32[]{:S(2)}) async-start(), calls=%async_computation.1 | async-start | bytes 3538944 | tf_op jit(solution)/shard_map/all_gather | solution.py:113
  10.7 98.1 %all-gather.11.cloned.1.call-start = ((), (), s32[]{:S(2)}) async-start(), calls=%async_computation.2 | async-start | bytes 3244032 | tf_op jit(solution)/shard_map/all_gather | solution.py:130
  61.5 28.5 %copy-start.2 = (s32[384]{0:T(512)S(1)}, s32[384]{0:T(512)}, u32[]{:S(2)}) copy-start(s32[384]{0:T(512)} %param.11) | copy-start | bytes 4612
  61.5 28.5 %copy-start.3 = (f32[384]{0:T(512)S(1)}, f32[384]{0:T(512)}, u32[]{:S(2)}) copy-start(f32[384]{0:T(512)} %param.12) | copy-start | bytes 4612
  61.5 100.9 %all-gather.7.cloned.1.call-start = ((), (), s32[]{:S(2)}) async-start(), calls=%async_computation | async-start | bytes 3244032 | tf_op jit(solution)/shard_map/all_gather | solution.py:129
Sparse Core Ops, SparseCore 0:
  10.9 47.0 all-gather.8
  61.6 47.1 all-gather.10
  111.3 51.0 all-gather.6
where the time goes:
time: 255 us; the launch traced here: 253 us
  waiting for transfers between devices  106 us (42%)
  matrix products  57.8 us (23%)
  other arithmetic  26.3 us (10%)
  blocking collectives  23.3 us (9%)
  local copies, waits for them, and re-layouts  15.5 us (6%)
  between operations  13.2 us (5%)
  loops' own time  10.8 us (4%)
    all_gather x1, waiting for transfers between devices, body(): lax.all_gather(key_rows, 'ctx', axis=0, tiled=True)  48.9 us
    all_gather x1, waiting for transfers between devices, body(): piece = lax.all_gather(picked, 'tp', axis=1, tiled=True)  47.2 us
    dot_general x8, matrix products, update(): jnp.einsum('hgrk,khd->rhgd', weights.astype(jnp.bfloat16), value_block, p...  25.2 us
    all_gather x1, blocking collectives, body(): lax.all_gather(position, 'ctx', axis=0, tiled=True)  23.3 us
    dot_general x8, matrix products, update(): jnp.einsum('rhgd,khd->hgrk', queries, key_block, preferred_element_type=j...  20.1 us
    reduce_sum x8, other arithmetic, update(): totals = totals * factor + jnp.sum(weights, axis=-1)  13.6 us
    another operation x1, loops' own time, fold_keys(): result, unused = lax.scan(advance, tuple(states), shaped)  10.4 us
    all_gather x1, waiting for transfers between devices, body(): lax.all_gather(value_rows, 'ctx', axis=0, tiled=True)  9.96 us
  transfers between devices with their start and end apart: 3, of which 3 were waited for; matrix products, arithmetic and copies ran while one was open for 7% of the time, Pallas kernels for 0%

commit v1 on v0

--- a/solution.py
+++ b/solution.py
@@ -96,6 +96,64 @@
     return result
 
 
+CODE_BASE = 64
+EXTRA_ROWS = 16
+
+
+def pack_payload(key_rows, value_rows, chosen):
+    slot_count = chosen.shape[0]
+    width = key_rows.shape[1] * key_rows.shape[2]
+    rows = jnp.concatenate(
+        [key_rows.reshape(slot_count, width), value_rows.reshape(slot_count, width)], axis=1
+    )
+    digits = jnp.concatenate(
+        [(chosen // CODE_BASE).reshape(-1, width), (chosen % CODE_BASE).reshape(-1, width)], axis=1
+    ).astype(jnp.bfloat16)
+    pad = jnp.zeros((EXTRA_ROWS - digits.shape[0], 2 * width), jnp.bfloat16)
+    return jnp.concatenate([rows, digits, pad], axis=0)
+
+
+def unpack_payload(payload, shards, slot_count, kv_local, head_dim):
+    width = kv_local * head_dim
+    blocks = payload.reshape(shards, slot_count + EXTRA_ROWS, 2 * width)
+    key_all = blocks[:, :slot_count, :width].reshape(shards * slot_count, kv_local, head_dim)
+    value_all = blocks[:, :slot_count, width:].reshape(shards * slot_count, kv_local, head_dim)
+    code_rows = slot_count // width
+    digits = blocks[:, slot_count : slot_count + code_rows, :].astype(jnp.int32)
+    chosen_all = digits[:, :, :width] * CODE_BASE + digits[:, :, width:]
+    return key_all, value_all, chosen_all.reshape(shards, slot_count)
+
+
+def ring_project(picked, weights, axis):
+    size = lax.axis_size(axis)
+    idx = lax.axis_index(axis)
+    width = picked.shape[1]
+    forward = [(i, (i + 1) % size) for i in range(size)]
+    backward = [(i, (i - 1) % size) for i in range(size)]
+
+    def partial(block, source):
+        start = source * width
+        return [
+            jnp.dot(block, lax.dynamic_slice_in_dim(w, start, width, axis=0), preferred_element_type=jnp.float32)
+            for w in weights
+        ]
+
+    sums = partial(picked, idx)
+    ahead = picked
+    behind = picked
+    steps_ahead = size // 2
+    steps_behind = size - 1 - steps_ahead
+    for step in range(1, steps_ahead + 1):
+        ahead = lax.ppermute(ahead, axis, forward)
+        parts = [partial(ahead, (idx - step) % size)]
+        if step <= steps_behind:
+            behind = lax.ppermute(behind, axis, backward)
+            parts.append(partial(behind, (idx + step) % size))
+        for part in parts:
+            sums = [s + p for s, p in zip(sums, part)]
+    return sums
+
+
 def body(hidden_states, chosen, router_gate, w_query, w_key, w_value):
     seq_rows = hidden_states.shape[0]
     slot_count = chosen.shape[0]
@@ -105,15 +163,13 @@
     kv_local = kv_width // head_dim
     heads_local = query_width // head_dim
     group = heads_local // kv_local
+    shards = lax.axis_size("ctx")
     live = chosen < seq_rows
-    pad_mark = lax.axis_size("ctx") * seq_rows + 1
+    pad_mark = shards * seq_rows + 1
     position = jnp.where(live, lax.axis_index("ctx") * seq_rows + chosen, pad_mark)
     picked = hidden_states[jnp.minimum(chosen, seq_rows - 1)]
     gated = jnp.where(live, router_gate, 0.0)
-    piece = lax.all_gather(picked, "tp", axis=1, tiled=True)
-    query_part = jnp.dot(piece, w_query, preferred_element_type=jnp.float32)
-    key_part = jnp.dot(piece, w_key, preferred_element_type=jnp.float32)
-    value_part = jnp.dot(piece, w_value, preferred_element_type=jnp.float32)
+    query_part, key_part, value_part = ring_project(picked, (w_query, w_key, w_value), "tp")
     queries = (
         rotate(query_part.reshape(slot_count, heads_local, head_dim), position) * head_dim ** (-0.5)
     ).astype(jnp.bfloat16)
@@ -122,14 +178,15 @@
         jnp.bfloat16
     )
     value_rows = value_part.reshape(slot_count, kv_local, head_dim).astype(jnp.bfloat16)
+    payload = pack_payload(key_rows, value_rows, chosen)
+    payload = lax.all_gather(payload, "ctx", axis=0, tiled=True)
+    key_all, value_all, chosen_all = unpack_payload(payload, shards, slot_count, kv_local, head_dim)
+    shard_base = (jnp.arange(shards, dtype=jnp.int32) * seq_rows)[:, None]
+    key_pos = jnp.where(chosen_all < seq_rows, shard_base + chosen_all, pad_mark).reshape(-1)
     groups = [(queries, position, highest(position, pad_mark))]
     states = fold_keys(
         (empty_state(slot_count, kv_local, group, head_dim),),
-        (
-            lax.all_gather(key_rows, "ctx", axis=0, tiled=True),
-            lax.all_gather(value_rows, "ctx", axis=0, tiled=True),
-            lax.all_gather(position, "ctx", axis=0, tiled=True),
-        ),
+        (key_all, value_all, key_pos),
         groups,
     )
     result = (finish(states[0]) * gated[:, None, None, None]).astype(jnp.bfloat16)

time: 255 us -> 212 us (0.83)
  waiting for transfers between devices: 106 us -> 65.6 us
  blocking collectives: 23.3 us -> 0 us
  starting transfers between devices: 0.09 us -> 12.6 us
  matrix products: 57.8 us -> 62.1 us
    all_gather x3 -> x1, waiting for transfers between devices: 106 us -> 44.5 us  [body(): payload = lax.all_gather(payload, 'ctx', axis=0, tiled=True)]
    all_gather x1 -> x0, blocking collectives: 23.3 us -> none  [body(): lax.all_gather(position, 'ctx', axis=0, tiled=True)]
    ppermute x0 -> x7, waiting for transfers between devices: none -> 21.1 us  [the longest x4 15 us: ring_project(): ahead = lax.ppermute(ahead, axis, forward)]
    ppermute x0 -> x7, starting transfers between devices: none -> 12.6 us  [the longest x3 10.8 us: ring_project(): behind = lax.ppermute(behind, axis, backward)]
    slice x0 -> x1, local copies, waits for them, and re-layouts: none -> 6.24 us  [unpack_payload(): blocks[:, :slot_count, width:]]
    while x2 -> x1, local copies, waits for them, and re-layouts: 9.28 us -> 4.88 us  [fold_keys(): result, unused = lax.scan(advance, tuple(states), shaped)]
    dot_general x3 -> x24, matrix products: 12.5 us -> 16.8 us  [partial(): jnp.dot(block, lax.dynamic_slice_in_dim(w, start, width, axis=0), preferr...]
  transfers between devices with their start and end apart: 3 -> 8, of which waited for: 3 -> 5; matrix products, arithmetic and copies ran while one was open for 7% -> 10% of each run, Pallas kernels for 0% -> 0%
where the time goes in v1:
time: 212 us; the launch traced here: 211 us
  waiting for transfers between devices  65.6 us (31%)
  matrix products  62.1 us (29%)
  other arithmetic  28.1 us (13%)
  local copies, waits for them, and re-layouts  18 us (8%)
  between operations  14 us (7%)
  starting transfers between devices  12.6 us (6%)
  loops' own time  10.4 us (5%)
    all_gather x1, waiting for transfers between devices, body(): payload = lax.all_gather(payload, 'ctx', axis=0, tiled=True)  44.5 us
    dot_general x8, matrix products, update(): jnp.einsum('hgrk,khd->rhgd', weights.astype(jnp.bfloat16), value_block, p...  25.3 us
    dot_general x8, matrix products, update(): jnp.einsum('rhgd,khd->hgrk', queries, key_block, preferred_element_type=j...  20.1 us
    dot_general x24, matrix products, partial(): jnp.dot(block, lax.dynamic_slice_in_dim(w, start, width, axis=0), preferr...  16.8 us
    ppermute x4, waiting for transfers between devices, ring_project(): ahead = lax.ppermute(ahead, axis, forward)  15 us
    reduce_sum x8, other arithmetic, update(): totals = totals * factor + jnp.sum(weights, axis=-1)  13.6 us
    ppermute x3, starting transfers between devices, ring_project(): behind = lax.ppermute(behind, axis, backward)  10.8 us
    another operation x1, loops' own time, fold_keys(): result, unused = lax.scan(advance, tuple(states), shaped)  9.99 us
  transfers between devices with their start and end apart: 8, of which 5 were waited for; matrix products, arithmetic and copies ran while one was open for 10% of the time, Pallas kernels for 0%

profile of v1, /device:TPU:31, one launch (start us, length us, event | category | flops | bytes accessed | tf_op | source)
XLA Modules:
  0.0 210.7 jit_solution(628647218466842141)
XLA Ops:
  11.9 4.0 %collective-permute-start.1 = (bf16[384,512]{1,0:T(8,128)(2,1)S(1)}, bf16[384,512]{1,0:T(8,128)(2,1)S(1)}, u32[]{:S(2)}, u32[]{:S(2)}) collective-permute-start(bf16[384,512]{1,0:T(8,128)(2,1)S(1)} %gather_fusion), channel_id=1, source_target_pairs={{0,7},{1,0},{2,1},{3,2},{4,3},{5,4},{6,5},{7,6},{8,15},{9,8},{10,9... | collective-permute-start | bytes 1179656 | tf_op jit(solution)/shard_map/ppermute | solution.py:150
  19.5 4.3 %collective-permute-done.1 = bf16[384,512]{1,0:T(8,128)(2,1)S(1)} collective-permute-done((bf16[384,512]{1,0:T(8,128)(2,1)S(1)}, bf16[384,512]{1,0:T(8,128)(2,1)S(1)}, u32[]{:S(2)}, u32[]{:S(2)}) %collective-permute-start.1) | collective-permute-done | bytes 393248 | tf_op jit(solution)/shard_map/ppermute | solution.py:150
  23.8 3.4 %collective-permute-start.3 = (bf16[384,512]{1,0:T(8,128)(2,1)S(1)}, bf16[384,512]{1,0:T(8,128)(2,1)S(1)}, u32[]{:S(2)}, u32[]{:S(2)}) collective-permute-start(bf16[384,512]{1,0:T(8,128)(2,1)S(1)} %collective-permute-done.1), channel_id=1, source_target_pairs={{0,7},{1,0},{2,1},{3,2},{4,3},{5,4},{6,5},{7,6},{8,15},{9,8},{10,9... | collective-permute-start | bytes 1179656 | tf_op jit(solution)/shard_map/ppermute | solution.py:150
  34.1 3.4 %collective-permute-start.5 = (bf16[384,512]{1,0:T(8,128)(2,1)S(1)}, bf16[384,512]{1,0:T(8,128)(2,1)S(1)}, u32[]{:S(2)}, u32[]{:S(2)}) collective-permute-start(bf16[384,512]{1,0:T(8,128)(2,1)S(1)} %collective-permute-done.3), channel_id=1, source_target_pairs={{0,7},{1,0},{2,1},{3,2},{4,3},{5,4},{6,5},{7,6},{8,15},{9,8},{10,9... | collective-permute-start | bytes 1179656 | tf_op jit(solution)/shard_map/ppermute | solution.py:150
  38.9 7.9 %collective-permute-done.4 = bf16[384,512]{1,0:T(8,128)(2,1)S(1)} collective-permute-done((bf16[384,512]{1,0:T(8,128)(2,1)S(1)}, bf16[384,512]{1,0:T(8,128)(2,1)S(1)}, u32[]{:S(2)}, u32[]{:S(2)}) %collective-permute-start.4) | collective-permute-done | bytes 393248 | tf_op jit(solution)/shard_map/ppermute | solution.py:147
  48.0 7.1 %collective-permute-done.6 = bf16[384,512]{1,0:T(8,128)(2,1)S(1)} collective-permute-done((bf16[384,512]{1,0:T(8,128)(2,1)S(1)}, bf16[384,512]{1,0:T(8,128)(2,1)S(1)}, u32[]{:S(2)}, u32[]{:S(2)}) %collective-permute-start.6) | collective-permute-done | bytes 393248 | tf_op jit(solution)/shard_map/ppermute | solution.py:147
  68.0 44.5 %all-gather.2.cloned.1.call-done = bf16[12800,256]{1,0:T(8,128)(2,1)} async-done(((bf16[400,256]{1,0:T(8,128)(2,1)}), bf16[12800,256]{1,0:T(8,128)(2,1)}) %all-gather.2.cloned.1.call-update) | async-done | bytes 6553616 | tf_op jit(solution)/shard_map/all_gather | solution.py:182
  112.5 6.2 %fusion.109 = (bf16[32,384,128]{2,1,0:T(8,128)(2,1)}, bf16[32,384,128]{2,1,0:T(8,128)(2,1)}) fusion(bf16[32,400,256]{2,1,0:T(8,128)(2,1)} %bitcast.113), kind=kLoop, calls=%fused_computation.157 | loop fusion | bytes 12582912 | tf_op jit(solution)/shard_map/slice | solution.py:120
  119.7 4.9 %copy.28 = bf16[8,1536,1,128]{1,3,2,0:T(8,128)(2,1)} copy(bf16[8,1536,1,128]{3,1,0,2:T(8,128)(2,1)} %bitcast.111) | data formatting | bytes 6291456 | tf_op jit(solution)/shard_map/while | solution.py:95
  124.8 78.0 %while.14 = (s32[]{:T(128)}, f32[1,4,384]{2,1,0:T(4,128)S(1)}, f32[1,4,384]{2,1,0:T(4,128)S(1)}, f32[384,1,4,128]{0,3,2,1:T(8,128)S(1)}, s32[8,1536]{1,0:T(8,128...) while((s32[]{:T(128)}, f32[1,4,384]{2,1,0:T(4,128)S(1)}, ...), condition=%wide.region_7.8_spmd, body=%wide.region_1.7_spmd.sunk | while | flops 1227823104 | bytes 33555200 | solution.py:95
  126.7 7.9 %conditional.2 = (f32[1,4,384]{2,1,0:T(4,128)S(1)}, f32[1,4,384]{2,1,0:T(4,128)S(1)}, f32[384,1,4,128]{0,3,2,1:T(8,128)S(1)}) conditional(s32[]{:T(128)} %convert_element_type.55, (s32[1,1536]{1,0:T(1,128)S(1)}, s32[384]{0:T(512)S(1)}, bf16[8,1536,1,128]{3,1,2,0:T(8,128)(2,1)}, s32[]{:T(128)}, bf16[384,1,4,128]{3,0,2,1:T(8,128)(2,1)S(1)}, ...), branch_computations={%region_3.5_spmd, %region_6.6_spmd} | conditional | flops 1227821568 | bytes 33530396 | solution.py:92
  127.1 2.5 %fusion = (f32[4,384]{1,0:T(4,128)S(1)}, f32[1536,384,4]{1,0,2:T(8,128)S(1)}) fusion(pred[384,1536]{0,1:T(8,128)(4,1)S(1)} %broadcast_compare_fusion, bf16[384,1,4,128]{3,0,2,1:T(8,128)(2,1)S(1)} %get-tuple-element.122, bf16[8,1536,1,128]{3,1,2,0:T(8,128)(2,1)} %get-tuple-element.120, s32[]{:T(128)} %get-tuple-element.121), kind=kOutput, calls=%fused_computation.3 | convolution fusion | flops 608696832 | bytes 10820096 | tf_op jit(solution)/shard_map/while/body/eval_jaxpr/cond/branch_0_fun/rhgd,khd->hgrk/dot_general | solution.py:40
  131.4 3.2 %fusion.12 = f32[384,1,4,128]{0,3,2,1:T(8,128)S(1)} fusion(f32[1536,384,4]{1,0,2:T(8,128)S(1)} %get-tuple-element.191, f32[4,384]{1,0:T(4,128)S(1)} %bitcast.116, pred[384,1536]{0,1:T(8,128)(4,1)S(1)} %broadcast_compare_fusion, f32[384,1,4,128]{0,3,2,1:T(8,128)S(1)} %get-tuple-element.124, bf16[8,1536,1,128]{1,3,2,0:T(8,128)(2,1)} %get-tuple-element.125, ...), kind=kOutput, calls=%fused_computation.12 | convolution fusion | flops 611450880 | bytes 12005888 | tf_op jit(solution)/shard_map/while/body/eval_jaxpr/cond/branch_0_fun/hgrk,khd->rhgd/dot_general | solution.py:46
  136.4 7.8 %conditional.2 = (f32[1,4,384]{2,1,0:T(4,128)S(1)}, f32[1,4,384]{2,1,0:T(4,128)S(1)}, f32[384,1,4,128]{0,3,2,1:T(8,128)S(1)}) conditional(s32[]{:T(128)} %convert_element_type.55, (s32[1,1536]{1,0:T(1,128)S(1)}, s32[384]{0:T(512)S(1)}, bf16[8,1536,1,128]{3,1,2,0:T(8,128)(2,1)}, s32[]{:T(128)}, bf16[384,1,4,128]{3,0,2,1:T(8,128)(2,1)S(1)}, ...), branch_computations={%region_3.5_spmd, %region_6.6_spmd} | conditional | flops 1227821568 | bytes 33530396 | solution.py:92
  141.1 3.2 %fusion.12 = f32[384,1,4,128]{0,3,2,1:T(8,128)S(1)} fusion(f32[1536,384,4]{1,0,2:T(8,128)S(1)} %get-tuple-element.191, f32[4,384]{1,0:T(4,128)S(1)} %bitcast.116, pred[384,1536]{0,1:T(8,128)(4,1)S(1)} %broadcast_compare_fusion, f32[384,1,4,128]{0,3,2,1:T(8,128)S(1)} %get-tuple-element.124, bf16[8,1536,1,128]{1,3,2,0:T(8,128)(2,1)} %get-tuple-element.125, ...), kind=kOutput, calls=%fused_computation.12 | convolution fusion | flops 611450880 | bytes 12005888 | tf_op jit(solution)/shard_map/while/body/eval_jaxpr/cond/branch_0_fun/hgrk,khd->rhgd/dot_general | solution.py:46
  146.2 7.9 %conditional.2 = (f32[1,4,384]{2,1,0:T(4,128)S(1)}, f32[1,4,384]{2,1,0:T(4,128)S(1)}, f32[384,1,4,128]{0,3,2,1:T(8,128)S(1)}) conditional(s32[]{:T(128)} %convert_element_type.55, (s32[1,1536]{1,0:T(1,128)S(1)}, s32[384]{0:T(512)S(1)}, bf16[8,1536,1,128]{3,1,2,0:T(8,128)(2,1)}, s32[]{:T(128)}, bf16[384,1,4,128]{3,0,2,1:T(8,128)(2,1)S(1)}, ...), branch_computations={%region_3.5_spmd, %region_6.6_spmd} | conditional | flops 1227821568 | bytes 33530396 | solution.py:92
  146.6 2.5 %fusion = (f32[4,384]{1,0:T(4,128)S(1)}, f32[1536,384,4]{1,0,2:T(8,128)S(1)}) fusion(pred[384,1536]{0,1:T(8,128)(4,1)S(1)} %broadcast_compare_fusion, bf16[384,1,4,128]{3,0,2,1:T(8,128)(2,1)S(1)} %get-tuple-element.122, bf16[8,1536,1,128]{3,1,2,0:T(8,128)(2,1)} %get-tuple-element.120, s32[]{:T(128)} %get-tuple-element.121), kind=kOutput, calls=%fused_computation.3 | convolution fusion | flops 608696832 | bytes 10820096 | tf_op jit(solution)/shard_map/while/body/eval_jaxpr/cond/branch_0_fun/rhgd,khd->hgrk/dot_general | solution.py:40
  150.9 3.2 %fusion.12 = f32[384,1,4,128]{0,3,2,1:T(8,128)S(1)} fusion(f32[1536,384,4]{1,0,2:T(8,128)S(1)} %get-tuple-element.191, f32[4,384]{1,0:T(4,128)S(1)} %bitcast.116, pred[384,1536]{0,1:T(8,128)(4,1)S(1)} %broadcast_compare_fusion, f32[384,1,4,128]{0,3,2,1:T(8,128)S(1)} %get-tuple-element.124, bf16[8,1536,1,128]{1,3,2,0:T(8,128)(2,1)} %get-tuple-element.125, ...), kind=kOutput, calls=%fused_computation.12 | convolution fusion | flops 611450880 | bytes 12005888 | tf_op jit(solution)/shard_map/while/body/eval_jaxpr/cond/branch_0_fun/hgrk,khd->rhgd/dot_general | solution.py:46
  155.9 7.8 %conditional.2 = (f32[1,4,384]{2,1,0:T(4,128)S(1)}, f32[1,4,384]{2,1,0:T(4,128)S(1)}, f32[384,1,4,128]{0,3,2,1:T(8,128)S(1)}) conditional(s32[]{:T(128)} %convert_element_type.55, (s32[1,1536]{1,0:T(1,128)S(1)}, s32[384]{0:T(512)S(1)}, bf16[8,1536,1,128]{3,1,2,0:T(8,128)(2,1)}, s32[]{:T(128)}, bf16[384,1,4,128]{3,0,2,1:T(8,128)(2,1)S(1)}, ...), branch_computations={%region_3.5_spmd, %region_6.6_spmd} | conditional | flops 1227821568 | bytes 33530396 | solution.py:92
  156.4 2.5 %fusion = (f32[4,384]{1,0:T(4,128)S(1)}, f32[1536,384,4]{1,0,2:T(8,128)S(1)}) fusion(pred[384,1536]{0,1:T(8,128)(4,1)S(1)} %broadcast_compare_fusion, bf16[384,1,4,128]{3,0,2,1:T(8,128)(2,1)S(1)} %get-tuple-element.122, bf16[8,1536,1,128]{3,1,2,0:T(8,128)(2,1)} %get-tuple-element.120, s32[]{:T(128)} %get-tuple-element.121), kind=kOutput, calls=%fused_computation.3 | convolution fusion | flops 608696832 | bytes 10820096 | tf_op jit(solution)/shard_map/while/body/eval_jaxpr/cond/branch_0_fun/rhgd,khd->hgrk/dot_general | solution.py:40
  160.6 3.2 %fusion.12 = f32[384,1,4,128]{0,3,2,1:T(8,128)S(1)} fusion(f32[1536,384,4]{1,0,2:T(8,128)S(1)} %get-tuple-element.191, f32[4,384]{1,0:T(4,128)S(1)} %bitcast.116, pred[384,1536]{0,1:T(8,128)(4,1)S(1)} %broadcast_compare_fusion, f32[384,1,4,128]{0,3,2,1:T(8,128)S(1)} %get-tuple-element.124, bf16[8,1536,1,128]{1,3,2,0:T(8,128)(2,1)} %get-tuple-element.125, ...), kind=kOutput, calls=%fused_computation.12 | convolution fusion | flops 611450880 | bytes 12005888 | tf_op jit(solution)/shard_map/while/body/eval_jaxpr/cond/branch_0_fun/hgrk,khd->rhgd/dot_general | solution.py:46
  165.7 7.9 %conditional.2 = (f32[1,4,384]{2,1,0:T(4,128)S(1)}, f32[1,4,384]{2,1,0:T(4,128)S(1)}, f32[384,1,4,128]{0,3,2,1:T(8,128)S(1)}) conditional(s32[]{:T(128)} %convert_element_type.55, (s32[1,1536]{1,0:T(1,128)S(1)}, s32[384]{0:T(512)S(1)}, bf16[8,1536,1,128]{3,1,2,0:T(8,128)(2,1)}, s32[]{:T(128)}, bf16[384,1,4,128]{3,0,2,1:T(8,128)(2,1)S(1)}, ...), branch_computations={%region_3.5_spmd, %region_6.6_spmd} | conditional | flops 1227821568 | bytes 33530396 | solution.py:92
  166.1 2.5 %fusion = (f32[4,384]{1,0:T(4,128)S(1)}, f32[1536,384,4]{1,0,2:T(8,128)S(1)}) fusion(pred[384,1536]{0,1:T(8,128)(4,1)S(1)} %broadcast_compare_fusion, bf16[384,1,4,128]{3,0,2,1:T(8,128)(2,1)S(1)} %get-tuple-element.122, bf16[8,1536,1,128]{3,1,2,0:T(8,128)(2,1)} %get-tuple-element.120, s32[]{:T(128)} %get-tuple-element.121), kind=kOutput, calls=%fused_computation.3 | convolution fusion | flops 608696832 | bytes 10820096 | tf_op jit(solution)/shard_map/while/body/eval_jaxpr/cond/branch_0_fun/rhgd,khd->hgrk/dot_general | solution.py:40
  170.4 3.2 %fusion.12 = f32[384,1,4,128]{0,3,2,1:T(8,128)S(1)} fusion(f32[1536,384,4]{1,0,2:T(8,128)S(1)} %get-tuple-element.191, f32[4,384]{1,0:T(4,128)S(1)} %bitcast.116, pred[384,1536]{0,1:T(8,128)(4,1)S(1)} %broadcast_compare_fusion, f32[384,1,4,128]{0,3,2,1:T(8,128)S(1)} %get-tuple-element.124, bf16[8,1536,1,128]{1,3,2,0:T(8,128)(2,1)} %get-tuple-element.125, ...), kind=kOutput, calls=%fused_computation.12 | convolution fusion | flops 611450880 | bytes 12005888 | tf_op jit(solution)/shard_map/while/body/eval_jaxpr/cond/branch_0_fun/hgrk,khd->rhgd/dot_general | solution.py:46
  175.5 7.8 %conditional.2 = (f32[1,4,384]{2,1,0:T(4,128)S(1)}, f32[1,4,384]{2,1,0:T(4,128)S(1)}, f32[384,1,4,128]{0,3,2,1:T(8,128)S(1)}) conditional(s32[]{:T(128)} %convert_element_type.55, (s32[1,1536]{1,0:T(1,128)S(1)}, s32[384]{0:T(512)S(1)}, bf16[8,1536,1,128]{3,1,2,0:T(8,128)(2,1)}, s32[]{:T(128)}, bf16[384,1,4,128]{3,0,2,1:T(8,128)(2,1)S(1)}, ...), branch_computations={%region_3.5_spmd, %region_6.6_spmd} | conditional | flops 1227821568 | bytes 33530396 | solution.py:92
  175.9 2.5 %fusion = (f32[4,384]{1,0:T(4,128)S(1)}, f32[1536,384,4]{1,0,2:T(8,128)S(1)}) fusion(pred[384,1536]{0,1:T(8,128)(4,1)S(1)} %broadcast_compare_fusion, bf16[384,1,4,128]{3,0,2,1:T(8,128)(2,1)S(1)} %get-tuple-element.122, bf16[8,1536,1,128]{3,1,2,0:T(8,128)(2,1)} %get-tuple-element.120, s32[]{:T(128)} %get-tuple-element.121), kind=kOutput, calls=%fused_computation.3 | convolution fusion | flops 608696832 | bytes 10820096 | tf_op jit(solution)/shard_map/while/body/eval_jaxpr/cond/branch_0_fun/rhgd,khd->hgrk/dot_general | solution.py:40
  180.1 3.2 %fusion.12 = f32[384,1,4,128]{0,3,2,1:T(8,128)S(1)} fusion(f32[1536,384,4]{1,0,2:T(8,128)S(1)} %get-tuple-element.191, f32[4,384]{1,0:T(4,128)S(1)} %bitcast.116, pred[384,1536]{0,1:T(8,128)(4,1)S(1)} %broadcast_compare_fusion, f32[384,1,4,128]{0,3,2,1:T(8,128)S(1)} %get-tuple-element.124, bf16[8,1536,1,128]{1,3,2,0:T(8,128)(2,1)} %get-tuple-element.125, ...), kind=kOutput, calls=%fused_computation.12 | convolution fusion | flops 611450880 | bytes 12005888 | tf_op jit(solution)/shard_map/while/body/eval_jaxpr/cond/branch_0_fun/hgrk,khd->rhgd/dot_general | solution.py:46
  185.2 7.9 %conditional.2 = (f32[1,4,384]{2,1,0:T(4,128)S(1)}, f32[1,4,384]{2,1,0:T(4,128)S(1)}, f32[384,1,4,128]{0,3,2,1:T(8,128)S(1)}) conditional(s32[]{:T(128)} %convert_element_type.55, (s32[1,1536]{1,0:T(1,128)S(1)}, s32[384]{0:T(512)S(1)}, bf16[8,1536,1,128]{3,1,2,0:T(8,128)(2,1)}, s32[]{:T(128)}, bf16[384,1,4,128]{3,0,2,1:T(8,128)(2,1)S(1)}, ...), branch_computations={%region_3.5_spmd, %region_6.6_spmd} | conditional | flops 1227821568 | bytes 33530396 | solution.py:92
  185.6 2.5 %fusion = (f32[4,384]{1,0:T(4,128)S(1)}, f32[1536,384,4]{1,0,2:T(8,128)S(1)}) fusion(pred[384,1536]{0,1:T(8,128)(4,1)S(1)} %broadcast_compare_fusion, bf16[384,1,4,128]{3,0,2,1:T(8,128)(2,1)S(1)} %get-tuple-element.122, bf16[8,1536,1,128]{3,1,2,0:T(8,128)(2,1)} %get-tuple-element.120, s32[]{:T(128)} %get-tuple-element.121), kind=kOutput, calls=%fused_computation.3 | convolution fusion | flops 608696832 | bytes 10820096 | tf_op jit(solution)/shard_map/while/body/eval_jaxpr/cond/branch_0_fun/rhgd,khd->hgrk/dot_general | solution.py:40
  189.9 3.2 %fusion.12 = f32[384,1,4,128]{0,3,2,1:T(8,128)S(1)} fusion(f32[1536,384,4]{1,0,2:T(8,128)S(1)} %get-tuple-element.191, f32[4,384]{1,0:T(4,128)S(1)} %bitcast.116, pred[384,1536]{0,1:T(8,128)(4,1)S(1)} %broadcast_compare_fusion, f32[384,1,4,128]{0,3,2,1:T(8,128)S(1)} %get-tuple-element.124, bf16[8,1536,1,128]{1,3,2,0:T(8,128)(2,1)} %get-tuple-element.125, ...), kind=kOutput, calls=%fused_computation.12 | convolution fusion | flops 611450880 | bytes 12005888 | tf_op jit(solution)/shard_map/while/body/eval_jaxpr/cond/branch_0_fun/hgrk,khd->rhgd/dot_general | solution.py:46
  195.0 7.8 %conditional.2 = (f32[1,4,384]{2,1,0:T(4,128)S(1)}, f32[1,4,384]{2,1,0:T(4,128)S(1)}, f32[384,1,4,128]{0,3,2,1:T(8,128)S(1)}) conditional(s32[]{:T(128)} %convert_element_type.55, (s32[1,1536]{1,0:T(1,128)S(1)}, s32[384]{0:T(512)S(1)}, bf16[8,1536,1,128]{3,1,2,0:T(8,128)(2,1)}, s32[]{:T(128)}, bf16[384,1,4,128]{3,0,2,1:T(8,128)(2,1)S(1)}, ...), branch_computations={%region_3.5_spmd, %region_6.6_spmd} | conditional | flops 1227821568 | bytes 33530396 | solution.py:92
  199.6 3.2 %fusion.12 = f32[384,1,4,128]{0,3,2,1:T(8,128)S(1)} fusion(f32[1536,384,4]{1,0,2:T(8,128)S(1)} %get-tuple-element.191, f32[4,384]{1,0:T(4,128)S(1)} %bitcast.116, pred[384,1536]{0,1:T(8,128)(4,1)S(1)} %broadcast_compare_fusion, f32[384,1,4,128]{0,3,2,1:T(8,128)S(1)} %get-tuple-element.124, bf16[8,1536,1,128]{1,3,2,0:T(8,128)(2,1)} %get-tuple-element.125, ...), kind=kOutput, calls=%fused_computation.12 | convolution fusion | flops 611450880 | bytes 12005888 | tf_op jit(solution)/shard_map/while/body/eval_jaxpr/cond/branch_0_fun/hgrk,khd->rhgd/dot_general | solution.py:46
  (152 shorter events, 60.4 us)
Async XLA Ops:
  6.5 1.6 copy-start
  6.5 106.0 %all-gather.2.cloned.1.call-start = ((), (), s32[]{:S(2)}) async-start(), calls=%async_computation | async-start | bytes 6758400 | tf_op jit(solution)/shard_map/all_gather | solution.py:182
  10.2 17.0 %collective-permute-start = (bf16[384,512]{1,0:T(8,128)(2,1)S(1)}, bf16[384,512]{1,0:T(8,128)(2,1)}, u32[]{:S(2)}, u32[]{:S(2)}) collective-permute-start(bf16[384,512]{1,0:T(8,128)(2,1)S(1)} %gather_fusion), channel_id=1, source_target_pairs={{0,1},{1,2},{2,3},{3,4},{4,5},{5,6},{6,7},{7,0},{8,9},{9,10},{10,1... | collective-permute-start | bytes 1179656 | tf_op jit(solution)/shard_map/ppermute | solution.py:147
  11.9 11.8 %collective-permute-start.1 = (bf16[384,512]{1,0:T(8,128)(2,1)S(1)}, bf16[384,512]{1,0:T(8,128)(2,1)S(1)}, u32[]{:S(2)}, u32[]{:S(2)}) collective-permute-start(bf16[384,512]{1,0:T(8,128)(2,1)S(1)} %gather_fusion), channel_id=1, source_target_pairs={{0,7},{1,0},{2,1},{3,2},{4,3},{5,4},{6,5},{7,6},{8,15},{9,8},{10,9... | collective-permute-start | bytes 1179656 | tf_op jit(solution)/shard_map/ppermute | solution.py:150
  18.0 19.5 %copy-start.10 = (bf16[4096,128]{1,0:T(8,128)(2,1)S(1)}, bf16[4096,128]{1,0:T(8,128)(2,1)}, u32[]{:S(2)}) copy-start(bf16[4096,128]{1,0:T(8,128)(2,1)} %param.14) | copy-start | bytes 3145732
  18.0 20.1 %copy-start.11 = (bf16[4096,128]{1,0:T(8,128)(2,1)S(1)}, bf16[4096,128]{1,0:T(8,128)(2,1)}, u32[]{:S(2)}) copy-start(bf16[4096,128]{1,0:T(8,128)(2,1)} %param.15) | copy-start | bytes 3145732
  23.8 8.5 %copy-start.2 = (bf16[384,512]{1,0:T(8,128)(2,1)}, bf16[384,512]{1,0:T(8,128)(2,1)S(1)}, u32[]{:S(2)}) copy-start(bf16[384,512]{1,0:T(8,128)(2,1)S(1)} %collective-permute-done.1) | copy-start | bytes 1179652
  23.8 10.4 %collective-permute-start.3 = (bf16[384,512]{1,0:T(8,128)(2,1)S(1)}, bf16[384,512]{1,0:T(8,128)(2,1)S(1)}, u32[]{:S(2)}, u32[]{:S(2)}) collective-permute-start(bf16[384,512]{1,0:T(8,128)(2,1)S(1)} %collective-permute-done.1), channel_id=1, source_target_pairs={{0,7},{1,0},{2,1},{3,2},{4,3},{5,4},{6,5},{7,6},{8,15},{9,8},{10,9... | collective-permute-start | bytes 1179656 | tf_op jit(solution)/shard_map/ppermute | solution.py:150
  27.2 10.4 %collective-permute-start.2 = (bf16[384,512]{1,0:T(8,128)(2,1)}, bf16[384,512]{1,0:T(8,128)(2,1)S(1)}, u32[]{:S(2)}, u32[]{:S(2)}) collective-permute-start(bf16[384,512]{1,0:T(8,128)(2,1)} %collective-permute-done), channel_id=1, source_target_pairs={{0,1},{1,2},{2,3},{3,4},{4,5},{5,6},{6,7},{7,0},{8,9},{9,10},{10,1... | collective-permute-start | bytes 1179656 | tf_op jit(solution)/shard_map/ppermute | solution.py:147
  34.1 12.6 %collective-permute-start.5 = (bf16[384,512]{1,0:T(8,128)(2,1)S(1)}, bf16[384,512]{1,0:T(8,128)(2,1)S(1)}, u32[]{:S(2)}, u32[]{:S(2)}) collective-permute-start(bf16[384,512]{1,0:T(8,128)(2,1)S(1)} %collective-permute-done.3), channel_id=1, source_target_pairs={{0,7},{1,0},{2,1},{3,2},{4,3},{5,4},{6,5},{7,6},{8,15},{9,8},{10,9... | collective-permute-start | bytes 1179656 | tf_op jit(solution)/shard_map/ppermute | solution.py:150
  37.5 1.3 copy-start.6
  37.5 9.2 %collective-permute-start.4 = (bf16[384,512]{1,0:T(8,128)(2,1)S(1)}, bf16[384,512]{1,0:T(8,128)(2,1)S(1)}, u32[]{:S(2)}, u32[]{:S(2)}) collective-permute-start(bf16[384,512]{1,0:T(8,128)(2,1)S(1)} %collective-permute-done.2), channel_id=1, source_target_pairs={{0,1},{1,2},{2,3},{3,4},{4,5},{5,6},{6,7},{7,0},{8,9},{9,10},{10,1... | collective-permute-start | bytes 1179656 | tf_op jit(solution)/shard_map/ppermute | solution.py:147
  37.9 18.4 %copy-start.13 = (bf16[3,256]{0,1:T(8,128)(2,1)S(1)}, bf16[3,256]{0,1:T(8,128)(2,1)}, u32[]{:S(2)}) copy-start(bf16[3,256]{0,1:T(8,128)(2,1)} %copy.23) | copy-start | bytes 4612
  38.5 18.7 %copy-start.14 = (s32[384]{0:T(512)S(1)}, s32[384]{0:T(512)}, u32[]{:S(2)}) copy-start(s32[384]{0:T(512)} %param.11) | copy-start | bytes 4612
  46.7 9.5 %copy-start.8 = (bf16[384,512]{1,0:T(8,128)(2,1)}, bf16[384,512]{1,0:T(8,128)(2,1)S(1)}, u32[]{:S(2)}) copy-start(bf16[384,512]{1,0:T(8,128)(2,1)S(1)} %collective-permute-done.4) | copy-start | bytes 1179652
  46.7 8.4 %collective-permute-start.6 = (bf16[384,512]{1,0:T(8,128)(2,1)S(1)}, bf16[384,512]{1,0:T(8,128)(2,1)S(1)}, u32[]{:S(2)}, u32[]{:S(2)}) collective-permute-start(bf16[384,512]{1,0:T(8,128)(2,1)S(1)} %collective-permute-done.4), channel_id=1, source_target_pairs={{0,1},{1,2},{2,3},{3,4},{4,5},{5,6},{6,7},{7,0},{8,9},{9,10},{10,1... | collective-permute-start | bytes 1179656 | tf_op jit(solution)/shard_map/ppermute | solution.py:147
  55.1 0.8 copy-start.4
  57.1 5.3 %copy-start.1 = (bf16[4096,512]{1,0:T(8,128)(2,1)S(1)}, bf16[4096,512]{1,0:T(8,128)(2,1)}, u32[]{:S(2)}) copy-start(bf16[4096,512]{1,0:T(8,128)(2,1)} %param.13) | copy-start | bytes 12582916
  57.2 5.3 %copy-start.3 = (bf16[384,512]{1,0:T(8,128)(2,1)S(1)}, bf16[384,512]{1,0:T(8,128)(2,1)}, u32[]{:S(2)}) copy-start(bf16[384,512]{1,0:T(8,128)(2,1)} %copy-done.2) | copy-start | bytes 1179652
  59.5 3.8 %copy-start.7 = (bf16[384,512]{1,0:T(8,128)(2,1)S(1)}, bf16[384,512]{1,0:T(8,128)(2,1)}, u32[]{:S(2)}) copy-start(bf16[384,512]{1,0:T(8,128)(2,1)} %copy-done.6) | copy-start | bytes 1179652
  62.5 1.6 copy-start.9
  63.3 1.2 copy-start.5
  64.4 3.1 %copy-start.12 = (f32[384,64]{1,0:T(8,128)S(1)}, f32[384,64]{1,0:T(8,128)}, u32[]{:S(2)}) copy-start(f32[384,64]{1,0:T(8,128)} %get-tuple-element.201) | copy-start | bytes 294916
Sparse Core Ops, SparseCore 0:
  57.3 55.2 all-gather.1

commit v2 on v1

v2 whole, which is shorter than its diff:
```python
import functools
import math

import jax
import jax.numpy as jnp
from jax import lax
from jax.experimental import pallas as pl
from jax.experimental.pallas import tpu as pltpu
from jax.sharding import PartitionSpec as P

HEAD_DIM = 128


ROPE_BASE = 500000.0
MASKED = -1e30
SUB = 128


def rotate(values_in, position):
    half_dim = values_in.shape[-1] // 2
    frequency = jnp.exp(
        jnp.arange(half_dim, dtype=jnp.float32) * (-2.0 * math.log(ROPE_BASE) / values_in.shape[-1])
    )
    angles = position.astype(jnp.float32)[:, None] * frequency[None, :]
    cosine = jnp.cos(angles)[:, None, :]
    sine = jnp.sin(angles)[:, None, :]
    first = values_in[..., :half_dim]
    second = values_in[..., half_dim:]
    return jnp.concatenate(
        [first * cosine - second * sine, second * cosine + first * sine], axis=-1
    )


def attend_kernel(scalars, q_ref, qpos_ref, gate_ref, kv_ref, kpos_ref, out_ref, m_scr, l_scr, acc_scr, *, q_rows, group, shards):
    t = pl.program_id(0)
    own = scalars[0]
    q_blocks = scalars[1]
    key_blocks = (scalars[2 + t] + (SUB - 1)) // SUB
    rows = group * SUB
    head_dim = q_ref.shape[1]

    @pl.when(t == 0)
    def _():
        m_scr[...] = jnp.full(m_scr.shape, MASKED, jnp.float32)
        l_scr[...] = jnp.zeros(l_scr.shape, jnp.float32)
        acc_scr[...] = jnp.zeros(acc_scr.shape, jnp.float32)

    for qb in range(q_rows // rows):
        for kb in range(kv_ref.shape[0] // SUB):
            @pl.when((t <= own) & (qb < q_blocks) & (kb < key_blocks))
            def _():
                r0, k0 = qb * rows, kb * SUB
                q = q_ref[r0:r0 + rows, :]
                k = kv_ref[k0:k0 + SUB, :head_dim]
                v = kv_ref[k0:k0 + SUB, head_dim:]
                s = lax.dot_general(q, k, (((1,), (1,)), ((), ())), preferred_element_type=jnp.float32)
                allowed = kpos_ref[:, k0:k0 + SUB] <= qpos_ref[r0:r0 + rows, :]
                m_prev = m_scr[r0:r0 + rows, :]
                m_cur = jnp.max(jnp.where(allowed, s, MASKED), axis=1, keepdims=True)
                m_new = jnp.maximum(m_prev, m_cur)
                alpha = jnp.exp(m_prev - m_new)
                p = jnp.where(allowed, jnp.exp(s - m_new[:, :1]), 0.0)
                l_scr[r0:r0 + rows, :] = alpha * l_scr[r0:r0 + rows, :] + jnp.sum(p, axis=1, keepdims=True)
                acc_scr[r0:r0 + rows, :] = alpha[:, :1] * acc_scr[r0:r0 + rows, :] + jnp.dot(
                    p.astype(jnp.bfloat16), v, preferred_element_type=jnp.float32
                )
                m_scr[r0:r0 + rows, :] = m_new

    @pl.when(t == shards - 1)
    def _():
        total = l_scr[...]
        denom = jnp.where(total > 0.0, total, 1.0)
        out_ref[...] = ((acc_scr[...] / denom) * gate_ref[...]).astype(out_ref.dtype)


def attend(scalars, q, qpos, gate, kv, kpos, interpret=False):
    q_rows, head_dim = q.shape
    shards, _, width = kv.shape
    slots = kpos.shape[2]
    group = q_rows // (slots)
    kernel = functools.partial(attend_kernel, q_rows=q_rows, group=group, shards=shards)

    def key_map(t, sc):
        return (jnp.minimum(t, sc[0]), 0, 0)

    grid_spec = pltpu.PrefetchScalarGridSpec(
        num_scalar_prefetch=1,
        grid=(shards,),
        in_specs=[
            pl.BlockSpec((q_rows, head_dim), lambda t, sc: (0, 0)),
            pl.BlockSpec((q_rows, 1), lambda t, sc: (0, 0)),
            pl.BlockSpec((q_rows, 1), lambda t, sc: (0, 0)),
            pl.BlockSpec((None, slots, width), key_map),
            pl.BlockSpec((None, 1, slots), key_map),
        ],
        out_specs=pl.BlockSpec((q_rows, head_dim), lambda t, sc: (0, 0)),
        scratch_shapes=[
            pltpu.VMEM((q_rows, 128), jnp.float32),
            pltpu.VMEM((q_rows, 128), jnp.float32),
            pltpu.VMEM((q_rows, head_dim), jnp.float32),
        ],
    )
    return pl.pallas_call(
        kernel,
        grid_spec=grid_spec,
        out_shape=jax.ShapeDtypeStruct((q_rows, head_dim), jnp.bfloat16),
        compiler_params=pltpu.CompilerParams(dimension_semantics=("arbitrary",)),
        interpret=interpret,
    )(scalars, q, qpos, gate, kv, kpos)


CODE_BASE = 64
EXTRA_ROWS = 16


def pack_payload(key_rows, value_rows, chosen):
    slot_count = chosen.shape[0]
    width = key_rows.shape[1] * key_rows.shape[2]
    rows = jnp.concatenate(
        [key_rows.reshape(slot_count, width), value_rows.reshape(slot_count, width)], axis=1
    )
    digits = jnp.concatenate(
        [(chosen // CODE_BASE).reshape(-1, width), (chosen % CODE_BASE).reshape(-1, width)], axis=1
    ).astype(jnp.bfloat16)
    pad = jnp.zeros((EXTRA_ROWS - digits.shape[0], 2 * width), jnp.bfloat16)
    return jnp.concatenate([rows, digits, pad], axis=0)


def unpack_chosen(blocks, slot_count, width):
    code_rows = slot_count // width
    digits = blocks[:, slot_count : slot_count + code_rows, :].astype(jnp.int32)
    chosen_all = digits[:, :, :width] * CODE_BASE + digits[:, :, width:]
    return chosen_all.reshape(blocks.shape[0], slot_count)


def ring_project(picked, weights, axis):
    size = lax.axis_size(axis)
    idx = lax.axis_index(axis)
    width = picked.shape[1]
    forward = [(i, (i + 1) % size) for i in range(size)]
    backward = [(i, (i - 1) % size) for i in range(size)]

    def partial(block, source):
        start = source * width
        return [
            jnp.dot(block, lax.dynamic_slice_in_dim(w, start, width, axis=0), preferred_element_type=jnp.float32)
            for w in weights
        ]

    sums = partial(picked, idx)
    ahead = picked
    behind = picked
    steps_ahead = size // 2
    steps_behind = size - 1 - steps_ahead
    for step in range(1, steps_ahead + 1):
        ahead = lax.ppermute(ahead, axis, forward)
        parts = [partial(ahead, (idx - step) % size)]
        if step <= steps_behind:
            behind = lax.ppermute(behind, axis, backward)
            parts.append(partial(behind, (idx + step) % size))
        for part in parts:
            sums = [s + p for s, p in zip(sums, part)]
    return sums


def body(hidden_states, chosen, router_gate, w_query, w_key, w_value):
    seq_rows = hidden_states.shape[0]
    slot_count = chosen.shape[0]
    head_dim = HEAD_DIM
    query_width = w_query.shape[1]
    kv_width = w_key.shape[1]
    kv_local = kv_width // head_dim
    heads_local = query_width // head_dim
    group = heads_local // kv_local
    shards = lax.axis_size("ctx")
    live = chosen < seq_rows
    pad_mark = shards * seq_rows + 1
    position = jnp.where(live, lax.axis_index("ctx") * seq_rows + chosen, pad_mark)
    picked = hidden_states[jnp.minimum(chosen, seq_rows - 1)]
    gated = jnp.where(live, router_gate, 0.0)
    query_part, key_part, value_part = ring_project(picked, (w_query, w_key, w_value), "tp")
    queries = (
        rotate(query_part.reshape(slot_count, heads_local, head_dim), position) * head_dim ** (-0.5)
    ).astype(jnp.bfloat16)
    key_rows = rotate(key_part.reshape(slot_count, kv_local, head_dim), position).astype(
        jnp.bfloat16
    )
    value_rows = value_part.reshape(slot_count, kv_local, head_dim).astype(jnp.bfloat16)
    payload = pack_payload(key_rows, value_rows, chosen)
    payload = lax.all_gather(payload, "ctx", axis=0, tiled=True)
    blocks = payload.reshape(shards, slot_count + EXTRA_ROWS, 2 * kv_width)
    chosen_all = unpack_chosen(blocks, slot_count, kv_width)
    shard_base = (jnp.arange(shards, dtype=jnp.int32) * seq_rows)[:, None]
    key_pos = jnp.where(chosen_all < seq_rows, shard_base + chosen_all, pad_mark)
    counts = jnp.sum((chosen_all < seq_rows).astype(jnp.int32), axis=1)
    q_blocks = (jnp.sum(live.astype(jnp.int32)) + (SUB - 1)) // SUB
    scalars = jnp.concatenate(
        [jnp.stack([lax.axis_index("ctx"), q_blocks]).astype(jnp.int32), counts]
    )
    q_tiles = slot_count // SUB
    flat_q = jnp.transpose(
        queries.reshape(q_tiles, SUB, group, head_dim), (0, 2, 1, 3)
    ).reshape(slot_count * group, head_dim)

    def per_row(values):
        spread = jnp.broadcast_to(values.reshape(q_tiles, 1, SUB), (q_tiles, group, SUB))
        return spread.reshape(slot_count * group, 1)

    out = attend(
        scalars, flat_q, per_row(position), per_row(gated), blocks, key_pos.reshape(shards, 1, slot_count)
    )
    out = jnp.transpose(out.reshape(q_tiles, group, SUB, head_dim), (0, 2, 1, 3))
    return out.reshape(slot_count, query_width)


def solution(mesh):
    placed = (P("ctx", "tp"), P("ctx"), P("ctx"), P(None, "tp"), P(None, "tp"), P(None, "tp"))
    return jax.shard_map(
        body, mesh=mesh, in_specs=placed, out_specs=P("ctx", "tp"), check_vma=False
    )
```

time: 212 us -> 245 us (1.16)
  the two profiles are of different devices: /device:TPU:31 before, /device:TPU:22 now
where the time goes in v2:
time: 245 us
  Pallas kernels  121 us (49%)
  waiting for transfers between devices  56.7 us (23%)
  matrix products  18.1 us (7%)
  between operations  14.6 us (6%)
  starting transfers between devices  13.4 us (5%)
  local copies, waits for them, and re-layouts  13.2 us (5%)
  other arithmetic  8.05 us (3%)
    pallas_call x1, Pallas kernels, attend(): pl.pallas_call(kernel, grid_spec=grid_spec, out_shape=jax.ShapeDtypeStruc...  121 us
    all_gather x1, waiting for transfers between devices, body(): payload = lax.all_gather(payload, 'ctx', axis=0, tiled=True)  32.8 us
    dot_general x24, matrix products, partial(): jnp.dot(block, lax.dynamic_slice_in_dim(w, start, width, axis=0), preferr...  18.1 us
    ppermute x4, waiting for transfers between devices, ring_project(): ahead = lax.ppermute(ahead, axis, forward)  16.7 us
    ppermute x3, starting transfers between devices, ring_project(): behind = lax.ppermute(behind, axis, backward)  11.4 us
    ppermute x3, waiting for transfers between devices, ring_project(): behind = lax.ppermute(behind, axis, backward)  7.24 us
  transfers between devices with their start and end apart: 8, of which 5 were waited for; matrix products, arithmetic and copies ran while one was open for 12% of the time, Pallas kernels for 0%

profile of v2, /device:TPU:22, one launch (start us, length us, event | category | flops | bytes accessed | tf_op | source)
XLA Modules:
  0.0 244.6 jit_solution(15612763473233976284)
XLA Ops:
  6.5 1.5 fusion.80
  8.1 2.1 gather_fusion
  10.2 2.0 collective-permute-start
  12.2 4.0 %collective-permute-start.1 = (bf16[384,512]{1,0:T(8,128)(2,1)S(1)}, bf16[384,512]{1,0:T(8,128)(2,1)S(1)}, u32[]{:S(2)}, u32[]{:S(2)}) collective-permute-start(bf16[384,512]{1,0:T(8,128)(2,1)S(1)} %gather_fusion), channel_id=1, source_target_pairs={{0,7},{1,0},{2,1},{3,2},{4,3},{5,4},{6,5},{7,6},{8,15},{9,8},{10,9... | collective-permute-start | bytes 1179656 | tf_op jit(solution)/shard_map/ppermute | solution.py:159
  16.2 1.2 fusion.45
  18.4 1.3 fusion.34
  19.8 4.8 %collective-permute-done.1 = bf16[384,512]{1,0:T(8,128)(2,1)S(1)} collective-permute-done((bf16[384,512]{1,0:T(8,128)(2,1)S(1)}, bf16[384,512]{1,0:T(8,128)(2,1)S(1)}, u32[]{:S(2)}, u32[]{:S(2)}) %collective-permute-start.1) | collective-permute-done | bytes 393248 | tf_op jit(solution)/shard_map/ppermute | solution.py:159
  24.6 3.7 %collective-permute-start.3 = (bf16[384,512]{1,0:T(8,128)(2,1)S(1)}, bf16[384,512]{1,0:T(8,128)(2,1)S(1)}, u32[]{:S(2)}, u32[]{:S(2)}) collective-permute-start(bf16[384,512]{1,0:T(8,128)(2,1)S(1)} %collective-permute-done.1), channel_id=1, source_target_pairs={{0,7},{1,0},{2,1},{3,2},{4,3},{5,4},{6,5},{7,6},{8,15},{9,8},{10,9... | collective-permute-start | bytes 1179656 | tf_op jit(solution)/shard_map/ppermute | solution.py:159
  28.3 1.3 convolution_add_fusion.14
  29.6 1.3 convolution_add_fusion.9
  31.0 1.2 convolution_add_fusion.13
  32.2 1.2 convolution_add_fusion.8
  33.4 2.4 collective-permute-done.3
  35.8 3.7 %collective-permute-start.5 = (bf16[384,512]{1,0:T(8,128)(2,1)S(1)}, bf16[384,512]{1,0:T(8,128)(2,1)S(1)}, u32[]{:S(2)}, u32[]{:S(2)}) collective-permute-start(bf16[384,512]{1,0:T(8,128)(2,1)S(1)} %collective-permute-done.3), channel_id=1, source_target_pairs={{0,7},{1,0},{2,1},{3,2},{4,3},{5,4},{6,5},{7,6},{8,15},{9,8},{10,9... | collective-permute-start | bytes 1179656 | tf_op jit(solution)/shard_map/ppermute | solution.py:159
  40.8 8.7 %collective-permute-done.4 = bf16[384,512]{1,0:T(8,128)(2,1)S(1)} collective-permute-done((bf16[384,512]{1,0:T(8,128)(2,1)S(1)}, bf16[384,512]{1,0:T(8,128)(2,1)S(1)}, u32[]{:S(2)}, u32[]{:S(2)}) %collective-permute-start.4) | collective-permute-done | bytes 393248 | tf_op jit(solution)/shard_map/ppermute | solution.py:156
  50.9 7.9 %collective-permute-done.6 = bf16[384,512]{1,0:T(8,128)(2,1)S(1)} collective-permute-done((bf16[384,512]{1,0:T(8,128)(2,1)S(1)}, bf16[384,512]{1,0:T(8,128)(2,1)S(1)}, u32[]{:S(2)}, u32[]{:S(2)}) %collective-permute-start.6) | collective-permute-done | bytes 393248 | tf_op jit(solution)/shard_map/ppermute | solution.py:156
  60.0 0.8 copy.21
  61.5 1.2 copy.27.qpos_ref
  63.4 1.2 copy.28.gate_ref
  65.0 1.6 fusion.19
  66.7 1.5 convolution_add_fusion.4
  68.2 1.4 convolution_add_fusion.3
  71.2 1.3 convolution_add_fusion
  72.5 1.4 copy.30
  74.0 0.8 multiply_subtract_fusion
  75.0 1.1 concatenate.38
  76.1 1.2 fusion.9
  77.3 2.0 copy.24
  79.3 32.8 %all-gather.2.cloned.1.call-done = bf16[12800,256]{1,0:T(8,128)(2,1)} async-done(((bf16[400,256]{1,0:T(8,128)(2,1)}), bf16[12800,256]{1,0:T(8,128)(2,1)}) %all-gather.2.cloned.1.call-update) | async-done | bytes 6553616 | tf_op jit(solution)/shard_map/all_gather | solution.py:190
  112.1 0.9 slice_convert_fusion
  115.1 120.6 %shard_map.64 = bf16[1536,128]{1,0:T(8,128)(2,1)} custom-call(s32[34]{0:T(128)} %pad_add_fusion.scalars, bf16[1536,128]{1,0:T(8,128)(2,1)} %bitcast.62, s32[1536,1]{1,0:T(8,128)} %copy.27.qpos_ref, f32[1536,1]{1,0:T(8,128)} %copy.28.gate_ref, bf16[32,400,256]{2,1,0:T(8,128)(2,1)} %bitcast.60, s32[32,1,384]{2,1,0:T(1,128)} %compare_select_fusion.kpos_ref), custom_call_target="tpu_custom_call" | custom-call | tf_op jit(solution)/shard_map/pallas_call | solution.py:103
  235.7 1.3 copy.29
  (67 shorter events, 10.3 us)
Async XLA Ops:
  6.5 1.6 copy-start
  6.5 105.5 %all-gather.2.cloned.1.call-start = ((), (), s32[]{:S(2)}) async-start(), calls=%async_computation | async-start | bytes 6758400 | tf_op jit(solution)/shard_map/all_gather | solution.py:190
  10.2 18.1 %collective-permute-start = (bf16[384,512]{1,0:T(8,128)(2,1)S(1)}, bf16[384,512]{1,0:T(8,128)(2,1)}, u32[]{:S(2)}, u32[]{:S(2)}) collective-permute-start(bf16[384,512]{1,0:T(8,128)(2,1)S(1)} %gather_fusion), channel_id=1, source_target_pairs={{0,1},{1,2},{2,3},{3,4},{4,5},{5,6},{6,7},{7,0},{8,9},{9,10},{10,1... | collective-permute-start | bytes 1179656 | tf_op jit(solution)/shard_map/ppermute | solution.py:156
  12.2 12.4 %collective-permute-start.1 = (bf16[384,512]{1,0:T(8,128)(2,1)S(1)}, bf16[384,512]{1,0:T(8,128)(2,1)S(1)}, u32[]{:S(2)}, u32[]{:S(2)}) collective-permute-start(bf16[384,512]{1,0:T(8,128)(2,1)S(1)} %gather_fusion), channel_id=1, source_target_pairs={{0,7},{1,0},{2,1},{3,2},{4,3},{5,4},{6,5},{7,6},{8,15},{9,8},{10,9... | collective-permute-start | bytes 1179656 | tf_op jit(solution)/shard_map/ppermute | solution.py:159
  18.3 21.2 %copy-start.9 = (bf16[4096,128]{1,0:T(8,128)(2,1)S(1)}, bf16[4096,128]{1,0:T(8,128)(2,1)}, u32[]{:S(2)}) copy-start(bf16[4096,128]{1,0:T(8,128)(2,1)} %param.10) | copy-start | bytes 3145732
  18.3 21.9 %copy-start.10 = (bf16[4096,128]{1,0:T(8,128)(2,1)S(1)}, bf16[4096,128]{1,0:T(8,128)(2,1)}, u32[]{:S(2)}) copy-start(bf16[4096,128]{1,0:T(8,128)(2,1)} %param.11) | copy-start | bytes 3145732
  24.6 8.8 %copy-start.2 = (bf16[384,512]{1,0:T(8,128)(2,1)}, bf16[384,512]{1,0:T(8,128)(2,1)S(1)}, u32[]{:S(2)}) copy-start(bf16[384,512]{1,0:T(8,128)(2,1)S(1)} %collective-permute-done.1) | copy-start | bytes 1179652
  24.6 11.2 %collective-permute-start.3 = (bf16[384,512]{1,0:T(8,128)(2,1)S(1)}, bf16[384,512]{1,0:T(8,128)(2,1)S(1)}, u32[]{:S(2)}, u32[]{:S(2)}) collective-permute-start(bf16[384,512]{1,0:T(8,128)(2,1)S(1)} %collective-permute-done.1), channel_id=1, source_target_pairs={{0,7},{1,0},{2,1},{3,2},{4,3},{5,4},{6,5},{7,6},{8,15},{9,8},{10,9... | collective-permute-start | bytes 1179656 | tf_op jit(solution)/shard_map/ppermute | solution.py:159
  28.3 11.2 %collective-permute-start.2 = (bf16[384,512]{1,0:T(8,128)(2,1)}, bf16[384,512]{1,0:T(8,128)(2,1)S(1)}, u32[]{:S(2)}, u32[]{:S(2)}) collective-permute-start(bf16[384,512]{1,0:T(8,128)(2,1)} %collective-permute-done), channel_id=1, source_target_pairs={{0,1},{1,2},{2,3},{3,4},{4,5},{5,6},{6,7},{7,0},{8,9},{9,10},{10,1... | collective-permute-start | bytes 1179656 | tf_op jit(solution)/shard_map/ppermute | solution.py:156
  35.8 13.8 %collective-permute-start.5 = (bf16[384,512]{1,0:T(8,128)(2,1)S(1)}, bf16[384,512]{1,0:T(8,128)(2,1)S(1)}, u32[]{:S(2)}, u32[]{:S(2)}) collective-permute-start(bf16[384,512]{1,0:T(8,128)(2,1)S(1)} %collective-permute-done.3), channel_id=1, source_target_pairs={{0,7},{1,0},{2,1},{3,2},{4,3},{5,4},{6,5},{7,6},{8,15},{9,8},{10,9... | collective-permute-start | bytes 1179656 | tf_op jit(solution)/shard_map/ppermute | solution.py:159
  39.5 1.3 copy-start.5
  39.5 10.1 %collective-permute-start.4 = (bf16[384,512]{1,0:T(8,128)(2,1)S(1)}, bf16[384,512]{1,0:T(8,128)(2,1)S(1)}, u32[]{:S(2)}, u32[]{:S(2)}) collective-permute-start(bf16[384,512]{1,0:T(8,128)(2,1)S(1)} %collective-permute-done.2), channel_id=1, source_target_pairs={{0,1},{1,2},{2,3},{3,4},{4,5},{5,6},{6,7},{7,0},{8,9},{9,10},{10,1... | collective-permute-start | bytes 1179656 | tf_op jit(solution)/shard_map/ppermute | solution.py:156
  39.8 20.1 %copy-start.11 = (bf16[3,256]{0,1:T(8,128)(2,1)S(1)}, bf16[3,256]{0,1:T(8,128)(2,1)}, u32[]{:S(2)}) copy-start(bf16[3,256]{0,1:T(8,128)(2,1)} %copy.20) | copy-start | bytes 4612
  40.5 22.2 %copy-start.12 = (s32[384]{0:T(512)S(1)}, s32[384]{0:T(512)}, u32[]{:S(2)}) copy-start(s32[384]{0:T(512)} %param.7) | copy-start | bytes 4612
  49.6 10.3 %copy-start.7 = (bf16[384,512]{1,0:T(8,128)(2,1)}, bf16[384,512]{1,0:T(8,128)(2,1)S(1)}, u32[]{:S(2)}) copy-start(bf16[384,512]{1,0:T(8,128)(2,1)S(1)} %collective-permute-done.4) | copy-start | bytes 1179652
  49.6 9.2 %collective-permute-start.6 = (bf16[384,512]{1,0:T(8,128)(2,1)S(1)}, bf16[384,512]{1,0:T(8,128)(2,1)S(1)}, u32[]{:S(2)}, u32[]{:S(2)}) collective-permute-start(bf16[384,512]{1,0:T(8,128)(2,1)S(1)} %collective-permute-done.4), channel_id=1, source_target_pairs={{0,1},{1,2},{2,3},{3,4},{4,5},{5,6},{6,7},{7,0},{8,9},{9,10},{10,1... | collective-permute-start | bytes 1179656 | tf_op jit(solution)/shard_map/ppermute | solution.py:156
  58.8 0.8 copy-start.3
  64.6 3.6 %copy-start.1 = (bf16[4096,512]{1,0:T(8,128)(2,1)S(1)}, bf16[4096,512]{1,0:T(8,128)(2,1)}, u32[]{:S(2)}) copy-start(bf16[4096,512]{1,0:T(8,128)(2,1)} %param.9) | copy-start | bytes 12582916
  65.0 5.0 %copy-start.6 = (bf16[384,512]{1,0:T(8,128)(2,1)S(1)}, bf16[384,512]{1,0:T(8,128)(2,1)}, u32[]{:S(2)}) copy-start(bf16[384,512]{1,0:T(8,128)(2,1)} %copy-done.5) | copy-start | bytes 1179652
  68.2 2.6 %copy-start.8 = (bf16[384,512]{1,0:T(8,128)(2,1)S(1)}, bf16[384,512]{1,0:T(8,128)(2,1)}, u32[]{:S(2)}) copy-start(bf16[384,512]{1,0:T(8,128)(2,1)} %copy-done.7) | copy-start | bytes 1179652
  70.0 1.2 copy-start.4
Sparse Core Ops, SparseCore 0:
  60.9 51.0 all-gather.1
